TPU v7x, 256 devices: a whole 4x4x8 slice. The times are simulated.
256 devices in a mesh: dp: 8 (over z), seq: 32 (over y, x, core).
Axes of the slice: x: 4, y: 4, z: 8, core: 2. Of those that a mesh axis runs over, the one named last changes fastest.
Arguments:
- inputs: bfloat16 [8, 4096, 2048], P('dp', 'seq'), may hold values from -6 to 6
- weight_codes: bfloat16 [2048, 1280], P('seq'), may hold values from -4 to 4
- scales: bfloat16 [2048, 10], P('seq'), may hold values from 0.010986328 to 0.043945312
- log_decay: float32 [8, 16, 4096], P('dp', None, 'seq'), may hold values from -0.85 to 0, as said below
- cotangent: bfloat16 [8, 4096, 1024], P('dp', 'seq'), may hold values from -6 to 6
Outputs:
- grad_inputs: float32 [8, 4096, 2048], P('dp', 'seq')
- grad_weight: float32 [2048, 1280], P('seq')
Inputs may be any that keep to these rules, and one draw needn't show every extreme that they name: log_decay is negative everywhere.
All inputs are finite; a program needn't handle non-finite values.
Results may differ from a plain program's by a relative error of at most 0.017.
Values may be sent and summed in bfloat16 or wider, within the bound.
No kernel may reach another device: no remote copies, remote signals or barrier semaphores. Data moves between devices by JAX's collectives and lax.ppermute only.
A program may use at most 128 MiB of HBM per device.

v0:
```python
import math
import jax
import jax.numpy as jnp
from jax import lax
from jax.sharding import PartitionSpec as P


def entering(part, axis, combine, identity, reverse):
    count = lax.axis_size(axis)
    place = lax.axis_index(axis)
    ahead = count - 1 - place if reverse else place
    gathered = jax.tree.map(lambda a: lax.all_gather(a, axis), part)
    state = jax.tree.map(lambda a, e: jnp.zeros_like(a) + jnp.asarray(e, a.dtype), part, identity)

    def one(hop, state):
        source = count - 1 - hop if reverse else hop
        return combine(
            state, jax.tree.map(lambda a: lax.dynamic_index_in_dim(a, source, 0, False), gathered)
        )

    return lax.fori_loop(0, ahead, one, state)


def dequantize(code_rows, scale_rows):
    row_count, col_count = code_rows.shape
    group_count = scale_rows.shape[1]
    spread = code_rows.astype(jnp.float32).reshape(row_count, group_count, col_count // group_count)
    spread = spread * scale_rows.astype(jnp.float32)[:, :, None]
    return spread.reshape(row_count, col_count).astype(jnp.bfloat16)


def block_prep(ld_block):
    cum_log = jnp.cumsum(ld_block, axis=1)
    input_scale = jnp.sqrt(-jnp.expm1(2.0 * ld_block))
    tail_weight = jnp.exp(cum_log[:, -1:] - cum_log) * input_scale
    return (cum_log, input_scale, tail_weight)


def weighted_pair(x_vals, grad_out, tail_weight, cum_log, inv_root):
    head_weight = jnp.exp(cum_log) * inv_root
    weighted_x = (x_vals.astype(jnp.float32) * tail_weight.T[:, :, None]).astype(jnp.bfloat16)
    weighted_g = (grad_out.astype(jnp.float32) * head_weight.T[:, :, None]).astype(jnp.bfloat16)
    return (weighted_x, weighted_g)


def summaries(x_vals, b_mat, c_mat, grad_out, ld_block):
    cum_log, input_scale, tail_weight = block_prep(ld_block)
    inv_root = 1.0 / math.sqrt(b_mat.shape[1])
    weighted_x, weighted_g = weighted_pair(x_vals, grad_out, tail_weight, cum_log, inv_root)
    fwd_state = jnp.einsum("sn,shp->hnp", b_mat, weighted_x, preferred_element_type=jnp.float32)
    back_state = jnp.einsum("tn,thp->hnp", c_mat, weighted_g, preferred_element_type=jnp.float32)
    return (jnp.exp(cum_log[:, -1]), fwd_state, back_state)


def block_grads(x_vals, b_mat, c_mat, grad_out, ld_block, state_in, back_in):
    block_len = ld_block.shape[1]
    cum_log, input_scale, tail_weight = block_prep(ld_block)
    inv_root = 1.0 / math.sqrt(b_mat.shape[1])
    weighted_x, weighted_g = weighted_pair(x_vals, grad_out, tail_weight, cum_log, inv_root)
    row_ids = lax.broadcasted_iota(jnp.int32, (block_len, block_len), 0)
    col_ids = lax.broadcasted_iota(jnp.int32, (block_len, block_len), 1)
    lower_mask = (row_ids >= col_ids)[None]
    log_gap = cum_log[:, :, None] - cum_log[:, None, :]
    decay_mat = jnp.where(lower_mask, jnp.exp(jnp.where(lower_mask, log_gap, 0.0)), 0.0)
    state_low = state_in.astype(jnp.bfloat16)
    back_low = back_in.astype(jnp.bfloat16)
    x_dot_g = jnp.einsum("thp,shp->hts", grad_out, x_vals, preferred_element_type=jnp.float32)
    c_dot_b = jnp.dot(c_mat, b_mat.T, preferred_element_type=jnp.float32)
    mix_weights = (
        jnp.sum(decay_mat * input_scale[:, None, :] * x_dot_g, axis=0) * inv_root
    ).astype(jnp.bfloat16)
    d_c = jnp.einsum("hnp,thp->tn", state_low, weighted_g, preferred_element_type=jnp.float32)
    d_c = d_c + jnp.dot(mix_weights, b_mat, preferred_element_type=jnp.float32)
    d_b = jnp.einsum("hnp,thp->tn", back_low, weighted_x, preferred_element_type=jnp.float32)
    d_b = d_b + jnp.dot(mix_weights.T, c_mat, preferred_element_type=jnp.float32)
    d_x = (
        jnp.einsum("tn,hnp->thp", b_mat, back_low, preferred_element_type=jnp.float32)
        * tail_weight.T[:, :, None]
    )
    inner_weights = (decay_mat * c_dot_b[None] * inv_root).astype(jnp.bfloat16)
    inner = jnp.einsum("hus,uhp->shp", inner_weights, grad_out, preferred_element_type=jnp.float32)
    d_x = d_x + input_scale.T[:, :, None] * inner
    return (d_x, d_b, d_c)


def state_chain(decays, adds, start, backward):

    def step(carry, item):
        return (item[0][:, None, None] * carry + item[1], carry)

    return lax.scan(step, start, (decays, adds), reverse=backward)


def join_summary(earlier, later):
    return (earlier[0] * later[0], later[0][:, None, None] * earlier[1] + later[1])


def local(inputs, weight_codes, scales, log_decay, cotangent):
    tok_count = inputs.shape[1]
    features = inputs[0]
    grad_out = cotangent[0]
    head_count = log_decay.shape[1]
    hp_width = grad_out.shape[1]
    head_dim = hp_width // head_count
    proj_width = weight_codes.shape[1]
    state_width = (proj_width - hp_width) // 2
    full_codes, full_scales = (
        lax.all_gather(weight_codes, "seq", axis=0, tiled=True),
        lax.all_gather(scales, "seq", axis=0, tiled=True),
    )
    weights = dequantize(full_codes, full_scales)
    projected = jnp.dot(features, weights, preferred_element_type=jnp.float32).astype(jnp.bfloat16)
    block_len = min(128, tok_count)
    block_count = tok_count // block_len
    x_blocks = projected[:, :hp_width].reshape(block_count, block_len, head_count, head_dim)
    b_blocks = projected[:, hp_width : hp_width + state_width].reshape(
        block_count, block_len, state_width
    )
    c_blocks = projected[:, hp_width + state_width :].reshape(block_count, block_len, state_width)
    g_blocks = grad_out.reshape(block_count, block_len, head_count, head_dim)
    ld_blocks = log_decay[0].reshape(head_count, block_count, block_len).transpose(1, 0, 2)
    decays, fwd_states, back_states = jax.vmap(summaries)(
        x_blocks, b_blocks, c_blocks, g_blocks, ld_blocks
    )
    zero_state = jnp.zeros((head_count, state_width, head_dim), jnp.float32)
    dev_decay = jnp.prod(decays, axis=0)
    dev_fwd, unused_a = state_chain(decays, fwd_states, zero_state, False)
    dev_back, unused_b = state_chain(decays, back_states, zero_state, True)
    neutral = (jnp.ones((head_count,), jnp.float32), zero_state)
    carried = entering((dev_decay, dev_fwd), "seq", join_summary, neutral, False)
    returned = entering((dev_decay, dev_back), "seq", join_summary, neutral, True)
    unused_c, state_starts = state_chain(decays, fwd_states, carried[1], False)
    unused_d, back_starts = state_chain(decays, back_states, returned[1], True)
    d_x, d_b, d_c = lax.map(
        lambda block_item: block_grads(*block_item),
        (x_blocks, b_blocks, c_blocks, g_blocks, ld_blocks, state_starts, back_starts),
    )
    d_proj = jnp.concatenate(
        [
            d_x.reshape(tok_count, hp_width),
            d_b.reshape(tok_count, state_width),
            d_c.reshape(tok_count, state_width),
        ],
        axis=1,
    ).astype(jnp.bfloat16)
    grad_in = lax.dot_general(
        d_proj, weights, (((1,), (1,)), ((), ())), preferred_element_type=jnp.float32
    )
    seq_count = lax.axis_size("seq")
    group_count = lax.axis_size("dp")
    norm_factor = 1.0 / math.sqrt(group_count * seq_count * tok_count)
    partial_grad = lax.psum_scatter(
        lax.dot_general(
            features, d_proj, (((0,), (0,)), ((), ())), preferred_element_type=jnp.float32
        ),
        "seq",
        scatter_dimension=0,
        tiled=True,
    )
    summed_grad = lax.psum(partial_grad, "dp")
    return (grad_in[None], summed_grad * norm_factor)


def solution(mesh):
    placed = (
        P("dp", "seq", None),
        P("seq", None),
        P("seq", None),
        P("dp", None, "seq"),
        P("dp", "seq", None),
    )
    return jax.shard_map(
        local,
        mesh=mesh,
        in_specs=placed,
        out_specs=(P("dp", "seq", None), P("seq", None)),
        check_vma=False,
    )
```

profile of v0, /device:TPU:2, one launch (start us, length us, event | category | flops | bytes accessed | tf_op | source)
XLA Modules:
  0.0 521.6 jit_solution(17085878530613788069)
XLA Ops:
  8.0 24.6 %all-gather.1 = bf16[32,64,10]{1,2,0:T(8,128)(2,1)S(1)} all-gather(bf16[1,64,10]{1,2,0:T(8,128)(2,1)} %bitcast.145), channel_id=1, replica_groups=mesh['dp'=8,'seq'=32] {'seq'}, dimensions={0}, use_global_device_ids=true | all-gather | bytes 42240 | tf_op jit(solution)/shard_map/all_gather | solution.py:109
  32.7 1.0 reduce_window_sum.23
  33.8 1.0 reduce_window_sum.24
  35.0 0.8 multiply_bitcast_fusion.3
  35.8 1.3 fusion.43
  37.1 28.6 %all-gather.6.cloned.1.call-done = bf16[2048,1280]{1,0:T(8,128)(2,1)} async-done(((bf16[64,1280]{1,0:T(8,128)(2,1)}), bf16[2048,1280]{1,0:T(8,128)(2,1)}) %all-gather.6.cloned.1.call-update) | async-done | bytes 5242896 | tf_op jit(solution)/shard_map/all_gather | solution.py:108
  65.7 7.9 %copy.59 = bf16[2048,1280]{0,1:T(8,128)(2,1)} copy(bf16[2048,1280]{1,0:T(8,128)(2,1)} %all-gather.6.cloned.1.call-done) | data formatting | bytes 10485760 | tf_op jit(solution)/shard_map/all_gather | solution.py:108
  73.6 3.9 fusion
  77.6 2.4 copy-done.2
  80.0 1.5 fusion.1
  81.5 0.8 fusion.15
  82.3 1.0 fusion.9
  83.6 0.8 fusion.13
  84.4 1.0 fusion.7
  85.5 21.4 %all-gather = f32[32,16,1]{1,2,0:T(1,128)} all-gather(f32[1,16,1]{1,2,0:T(1,128)S(1)} %exp.58), channel_id=2, replica_groups=mesh['dp'=8,'seq'=32] {'seq'}, dimensions={0}, use_global_device_ids=true | all-gather | bytes 2112 | tf_op jit(solution)/shard_map/all_gather | solution.py:12
  106.9 0.9 fusion.3
  107.8 0.8 fusion.29
  108.7 52.1 %all-gather.10.cloned.1.call-done = f32[32,16,128,64]{2,3,1,0:T(8,128)} async-done(((f32[1,16,128,64]{2,3,1,0:T(8,128)}), f32[32,16,128,64]{2,3,1,0:T(8,128)}) %all-gather.10.cloned.1.call-update) | async-done | bytes 16777232 | tf_op jit(solution)/shard_map/all_gather | solution.py:12
  160.9 4.7 while.17
  160.9 1.1 constant_dynamic-slice_fusion.5
  163.3 1.1 constant_dynamic-slice_fusion.5
  165.6 74.8 %all-gather.8.cloned.1.call-done = f32[32,16,128,64]{2,3,1,0:T(8,128)} async-done(((f32[1,16,128,64]{2,3,1,0:T(8,128)}), f32[32,16,128,64]{2,3,1,0:T(8,128)}) %all-gather.8.cloned.1.call-update) | async-done | bytes 16777232 | tf_op jit(solution)/shard_map/all_gather | solution.py:12
  240.5 68.7 %while.16 = (s32[]{:T(128)}, f32[16,128,64]{2,1,0:T(8,128)S(1)}, s32[]{:T(128)}, f32[32,16]{1,0:T(8,128)}, f32[32,16,128,64]{2,3,1,0:T(8,128)}, /*index=5*/s32[]{:T(128)}, s32[]{:T(128)}, s32[]{:T(128)}, s32[]{:T(128)}) while((s32[]{:T(128)}, f32[16,128,64]{2,1,0:T(8,128)S(1)}, s32[]{:T(128)}, f32[32,16]{1,0:T(8,128)}, ...), condition=%wide.region_2.3_spmd, body=%wide.region_1.2_spmd.sunk | while | flops 262150 | bytes 3670363 | solution.py:21
  240.6 1.1 constant_dynamic-slice_fusion.4
  242.0 0.7 dynamic-slice_bitcast_fusion.4
  242.9 1.1 constant_dynamic-slice_fusion.4
  245.3 1.1 constant_dynamic-slice_fusion.4
  247.7 1.1 constant_dynamic-slice_fusion.4
  250.1 1.1 constant_dynamic-slice_fusion.4
  252.4 1.1 constant_dynamic-slice_fusion.4
  253.9 0.7 dynamic-slice_bitcast_fusion.4
  254.8 1.1 constant_dynamic-slice_fusion.4
  257.2 1.1 constant_dynamic-slice_fusion.4
  259.5 1.1 constant_dynamic-slice_fusion.4
  261.9 1.1 constant_dynamic-slice_fusion.4
  264.3 1.1 constant_dynamic-slice_fusion.4
  266.6 1.1 constant_dynamic-slice_fusion.4
  269.0 1.1 constant_dynamic-slice_fusion.4
  271.4 1.1 constant_dynamic-slice_fusion.4
  273.7 1.1 constant_dynamic-slice_fusion.4
  276.1 1.1 constant_dynamic-slice_fusion.4
  278.4 1.1 constant_dynamic-slice_fusion.4
  280.8 1.1 constant_dynamic-slice_fusion.4
  283.2 1.1 constant_dynamic-slice_fusion.4
  285.6 1.1 constant_dynamic-slice_fusion.4
  287.9 1.1 constant_dynamic-slice_fusion.4
  290.3 1.1 constant_dynamic-slice_fusion.4
  292.7 1.1 constant_dynamic-slice_fusion.4
  295.0 1.1 constant_dynamic-slice_fusion.4
  297.4 1.1 constant_dynamic-slice_fusion.4
  299.8 1.1 constant_dynamic-slice_fusion.4
  302.1 1.1 constant_dynamic-slice_fusion.4
  304.5 1.1 constant_dynamic-slice_fusion.4
  306.9 1.1 constant_dynamic-slice_fusion.4
  309.6 1.2 convolution_bitcast_fusion.7
  310.8 1.5 convolution_bitcast_fusion.6
  313.5 5.3 %convolution_bitcast_fusion = f32[2048,1280]{0,1:T(8,128)} fusion(bf16[1,128,2048]{2,1,0:T(8,128)(2,1)S(1)} %copy-done, bf16[128,128]{0,1:T(8,128)(2,1)S(1)} %fusion.12, bf16[128,128]{0,1:T(8,128)(2,1)S(1)} %fusion.11, bf16[128,1024]{0,1:T(8,128)(2,1)S(1)} %bitcast.132), kind=kOutput, calls=%fused_computation.8 | convolution fusion | flops 672071680 | bytes 11337728 | tf_op jit(solution)/shard_map/dot_general | solution.py:153
  318.9 11.3 %copy.89 = f32[2048,1280]{1,0:T(8,128)} copy(f32[2048,1280]{0,1:T(8,128)} %convolution_bitcast_fusion) | data formatting | bytes 20971520
  330.2 106.7 %reduce-scatter.4.cloned.1.call-done = f32[64,1280]{1,0:T(8,128)} async-done(((f32[2048,1280]{1,0:T(8,128)}), f32[64,1280]{1,0:T(8,128)}) %reduce-scatter.4.cloned.1.call-update) | async-done | bytes 327696
  436.9 2.1 copy.90
  439.0 4.3 convolution_bitcast_fusion.1
  443.4 69.7 %all-reduce.2.cloned.1.call-done = f32[64,1280]{0,1:T(8,128)} async-done(((f32[64,1280]{0,1:T(8,128)}), f32[64,1280]{0,1:T(8,128)}) %all-reduce.2.cloned.1.call-update) | async-done | bytes 327696 | tf_op jit(solution)/shard_map/psum | solution.py:160
  513.0 1.1 broadcast_multiply_fusion
  514.2 0.9 copy.77
  (138 shorter events, 40.5 us)
Async XLA Ops:
  7.2 72.8 %copy-start = (bf16[1,128,2048]{2,1,0:T(8,128)(2,1)S(1)}, bf16[1,128,2048]{2,1,0:T(8,128)(2,1)}, u32[]{:S(2)}) copy-start(bf16[1,128,2048]{2,1,0:T(8,128)(2,1)} %param.9) | copy-start | bytes 1572868
  7.2 58.5 %all-gather.6.cloned.1.call-start = ((), (), s32[]{:S(2)}) async-start(), calls=%async_computation.1 | async-start | bytes 5406720 | tf_op jit(solution)/shard_map/all_gather | solution.py:108
  7.9 152.9 %all-gather.10.cloned.1.call-start = ((), (), s32[]{:S(2)}) async-start(), calls=%async_computation.3 | async-start | bytes 17301504 | tf_op jit(solution)/shard_map/all_gather | solution.py:12
  77.6 2.4 copy-start.2
  79.9 3.4 copy-start.5
  83.3 157.1 %all-gather.8.cloned.1.call-start = ((), (), s32[]{:S(2)}) async-start(), calls=%async_computation.2 | async-start | bytes 17301504 | tf_op jit(solution)/shard_map/all_gather | solution.py:12
  83.6 77.2 %copy-start.3 = (bf16[1,128,1024]{1,2,0:T(8,128)(2,1)}, bf16[1,128,1024]{1,2,0:T(8,128)(2,1)S(1)}, u32[]{:S(2)}) copy-start(bf16[1,128,1024]{1,2,0:T(8,128)(2,1)S(1)} %copy.63) | copy-start | bytes 786436
  85.4 351.5 %reduce-scatter.4.cloned.1.call-start = ((), (), s32[]{:S(2)}) async-start(), calls=%async_computation.5 | async-start | bytes 10813440
  106.9 53.9 %copy-start.7 = (pred[128,128]{0,1:T(8,128)(4,1)}, pred[128,128]{0,1:T(8,128)(4,1)S(1)}, u32[]{:S(2)}) copy-start(pred[128,128]{0,1:T(8,128)(4,1)S(1)} %iota_compare_fusion) | copy-start | bytes 49156
  165.6 74.9 %copy-start.1 = (f32[16,128,64]{2,1,0:T(8,128)}, f32[16,128,64]{2,1,0:T(8,128)S(1)}, u32[]{:S(2)}) copy-start(f32[16,128,64]{2,1,0:T(8,128)S(1)} %get-tuple-element.218) | copy-start | bytes 1572868
  309.2 3.7 copy-start.4
  309.2 3.7 copy-start.6
  309.2 3.7 copy-start.8
  309.3 3.7 copy-start.9
  330.2 182.8 %all-reduce.2.cloned.1.call-start = ((), (), s32[]{:S(2)}) async-start(), calls=%async_computation.4 | async-start | bytes 1310720 | tf_op jit(solution)/shard_map/psum | solution.py:160
Sparse Core Ops, SparseCore 0:
  10.6 55.0 all-gather.5
  83.4 77.2 all-gather.9
  163.3 77.0 all-gather.7
  330.3 106.5 reduce-scatter.3
  439.2 73.7 all-reduce.1
where the time goes:
time: 525 us; the launch traced here: 522 us
  waiting for transfers between devices  333 us (63%)
  local copies, waits for them, and re-layouts  91.1 us (17%)
  blocking collectives  46 us (9%)
  matrix products  18.9 us (4%)
  other arithmetic  17.6 us (3%)
  between operations  14 us (3%)
    all_gather x2, waiting for transfers between devices, entering(): gathered = jax.tree.map(lambda a: lax.all_gather(a, axis), part)  127 us
    unnamed x6, waiting for transfers between devices  107 us
    psum x1, waiting for transfers between devices, local(): summed_grad = lax.psum(partial_grad, 'dp')  69.7 us
    dynamic_slice x62, local copies, waits for them, and re-layouts, one(): lax.dynamic_index_in_dim(a, source, 0, False)  43.9 us
    all_gather x1, waiting for transfers between devices, local(): lax.all_gather(weight_codes, 'seq', axis=0, tiled=True)  28.6 us
    all_gather x1, blocking collectives, local(): lax.all_gather(scales, 'seq', axis=0, tiled=True)  24.6 us
    mul x31, local copies, waits for them, and re-layouts, join_summary(): later[0][:, None, None] * earlier[1] + later[1]  21.4 us
    all_gather x1, blocking collectives, entering(): gathered = jax.tree.map(lambda a: lax.all_gather(a, axis), part)  21.4 us
  transfers between devices with their start and end apart: 5, of which 5 were waited for; matrix products, arithmetic and copies ran while one was open for 3% of the time, Pallas kernels for 0%

commit v1 on v0

--- a/solution.py
+++ b/solution.py
@@ -157,7 +157,7 @@
         scatter_dimension=0,
         tiled=True,
     )
-    summed_grad = lax.psum(partial_grad, "dp")
+    summed_grad = jnp.sum(lax.all_gather(partial_grad, "dp"), axis=0)
     return (grad_in[None], summed_grad * norm_factor)
 
 

time: 525 us -> 563 us (1.072)
  other arithmetic: 17.6 us -> 82.5 us
  waiting for transfers between devices: 333 us -> 307 us
    reduce_scatter x0 -> x1, waiting for transfers between devices: none -> 111 us  [local(): lax.psum_scatter(lax.dot_general(features, d_proj, (((0,), (0,)), ((), ()...]
    unnamed x6 -> x5, waiting for transfers between devices: 107 us -> 0.75 us
    psum x1 -> x0, waiting for transfers between devices: 69.7 us -> none  [local(): summed_grad = lax.psum(partial_grad, 'dp')]
    add x31, other arithmetic: 6.79 us -> 68.9 us  [join_summary(): later[0][:, None, None] * earlier[1] + later[1]]
    all_gather x0 -> x1, waiting for transfers between devices: none -> 39.4 us  [local(): summed_grad = jnp.sum(lax.all_gather(partial_grad, 'dp'), axis=0)]
    unnamed x25 -> x15, local copies, waits for them, and re-layouts: 17 us -> 13.9 us
where the time goes in v1:
time: 563 us; the launch traced here: 558 us
  waiting for transfers between devices  307 us (55%)
  local copies, waits for them, and re-layouts  88.8 us (16%)
  other arithmetic  82.5 us (15%)
  blocking collectives  45.7 us (8%)
  matrix products  19.4 us (3%)
  between operations  14 us (2%)
    all_gather x2, waiting for transfers between devices, entering(): gathered = jax.tree.map(lambda a: lax.all_gather(a, axis), part)  127 us
    reduce_scatter x1, waiting for transfers between devices, local(): lax.psum_scatter(lax.dot_general(features, d_proj, (((0,), (0,)), ((), ()...  111 us
    add x31, other arithmetic, join_summary(): later[0][:, None, None] * earlier[1] + later[1]  68.9 us
    dynamic_slice x62, local copies, waits for them, and re-layouts, one(): lax.dynamic_index_in_dim(a, source, 0, False)  43.8 us
    all_gather x1, waiting for transfers between devices, local(): summed_grad = jnp.sum(lax.all_gather(partial_grad, 'dp'), axis=0)  39.4 us
    all_gather x1, waiting for transfers between devices, local(): lax.all_gather(weight_codes, 'seq', axis=0, tiled=True)  28.6 us
    all_gather x1, blocking collectives, local(): lax.all_gather(scales, 'seq', axis=0, tiled=True)  24.6 us
    mul x31, local copies, waits for them, and re-layouts, join_summary(): later[0][:, None, None] * earlier[1] + later[1]  21.4 us
  transfers between devices with their start and end apart: 5, of which 5 were waited for; matrix products, arithmetic and copies ran while one was open for 3% of the time, Pallas kernels for 0%

profile of v1, /device:TPU:2, one launch (start us, length us, event | category | flops | bytes accessed | tf_op | source)
XLA Modules:
  0.0 557.9 jit_solution(12936653987714417815)
XLA Ops:
  8.0 24.6 %all-gather.2 = bf16[32,64,10]{1,2,0:T(8,128)(2,1)S(1)} all-gather(bf16[1,64,10]{1,2,0:T(8,128)(2,1)} %bitcast.147), channel_id=1, replica_groups=mesh['dp'=8,'seq'=32] {'seq'}, dimensions={0}, use_global_device_ids=true | all-gather | bytes 42240 | tf_op jit(solution)/shard_map/all_gather | solution.py:109
  35.8 1.3 fusion.43
  37.1 28.6 %all-gather.8.cloned.1.call-done = bf16[2048,1280]{1,0:T(8,128)(2,1)} async-done(((bf16[64,1280]{1,0:T(8,128)(2,1)}), bf16[2048,1280]{1,0:T(8,128)(2,1)}) %all-gather.8.cloned.1.call-update) | async-done | bytes 5242896 | tf_op jit(solution)/shard_map/all_gather | solution.py:108
  65.7 8.0 %copy.58 = bf16[2048,1280]{0,1:T(8,128)(2,1)} copy(bf16[2048,1280]{1,0:T(8,128)(2,1)} %all-gather.8.cloned.1.call-done) | data formatting | bytes 10485760 | tf_op jit(solution)/shard_map/all_gather | solution.py:108
  73.6 3.9 fusion
  77.6 2.4 copy-done.1
  79.9 1.5 fusion.1
  85.5 21.1 %all-gather = f32[32,16,1]{1,2,0:T(1,128)} all-gather(f32[1,16,1]{1,2,0:T(1,128)S(1)} %exp.58), channel_id=2, replica_groups=mesh['dp'=8,'seq'=32] {'seq'}, dimensions={0}, use_global_device_ids=true | all-gather | bytes 2112 | tf_op jit(solution)/shard_map/all_gather | solution.py:12
  108.4 52.5 %all-gather.12.cloned.1.call-done = f32[32,16,128,64]{2,3,1,0:T(8,128)} async-done(((f32[1,16,128,64]{2,3,1,0:T(8,128)}), f32[32,16,128,64]{2,3,1,0:T(8,128)}) %all-gather.12.cloned.1.call-update) | async-done | bytes 16777232 | tf_op jit(solution)/shard_map/all_gather | solution.py:12
  161.0 4.7 while.17
  161.0 1.1 constant_dynamic-slice_fusion.5
  163.3 1.1 constant_dynamic-slice_fusion.5
  165.7 74.8 %all-gather.10.cloned.1.call-done = f32[32,16,128,64]{2,3,1,0:T(8,128)} async-done(((f32[1,16,128,64]{2,3,1,0:T(8,128)}), f32[32,16,128,64]{2,3,1,0:T(8,128)}) %all-gather.10.cloned.1.call-update) | async-done | bytes 16777232 | tf_op jit(solution)/shard_map/all_gather | solution.py:12
  240.5 1.1 broadcast_in_dim.76.clone.1
  241.6 129.8 %while.16 = (s32[]{:T(128)}, f32[16,128,64]{2,1,0:T(8,128)}, s32[]{:T(128)}, f32[32,16]{1,0:T(8,128)}, f32[32,16,128,64]{2,3,1,0:T(8,128)}, /*index=5*/s32[]{:T(128)}, s32[]{:T(128)}, s32[]{:T(128)}, s32[]{:T(128)}) while((s32[]{:T(128)}, f32[16,128,64]{2,1,0:T(8,128)}, s32[]{:T(128)}, f32[32,16]{1,0:T(8,128)}, f32[32,16,128,64]{2,3,1,0:T(8,128)}, ...), condition=%wide.region_2.3_spmd, body=%wide.region_1.2_spmd.sunk | while | flops 262150 | bytes 3670363 | solution.py:21
  241.6 1.1 constant_dynamic-slice_fusion.4
  243.7 2.4 bitcast_add_fusion.4
  246.1 1.1 constant_dynamic-slice_fusion.4
  248.2 2.4 bitcast_add_fusion.4
  250.5 1.1 constant_dynamic-slice_fusion.4
  252.7 2.4 bitcast_add_fusion.4
  255.0 1.1 constant_dynamic-slice_fusion.4
  257.1 2.4 bitcast_add_fusion.4
  261.6 2.4 bitcast_add_fusion.4
  266.1 2.4 bitcast_add_fusion.4
  268.5 1.1 constant_dynamic-slice_fusion.4
  270.6 2.4 bitcast_add_fusion.4
  275.1 2.4 bitcast_add_fusion.4
  279.5 2.4 bitcast_add_fusion.4
  284.0 2.4 bitcast_add_fusion.4
  288.5 2.4 bitcast_add_fusion.4
  293.0 2.4 bitcast_add_fusion.4
  297.5 2.4 bitcast_add_fusion.4
  302.0 2.4 bitcast_add_fusion.4
  306.4 2.4 bitcast_add_fusion.4
  310.9 2.4 bitcast_add_fusion.4
  315.4 2.4 bitcast_add_fusion.4
  317.7 1.1 constant_dynamic-slice_fusion.4
  319.8 2.4 bitcast_add_fusion.4
  324.3 2.4 bitcast_add_fusion.4
  328.8 2.4 bitcast_add_fusion.4
  331.1 1.1 constant_dynamic-slice_fusion.4
  333.2 2.4 bitcast_add_fusion.4
  337.7 2.4 bitcast_add_fusion.4
  342.1 2.4 bitcast_add_fusion.4
  344.5 1.1 constant_dynamic-slice_fusion.4
  346.6 2.4 bitcast_add_fusion.4
  351.1 2.4 bitcast_add_fusion.4
  355.5 2.4 bitcast_add_fusion.4
  360.0 2.4 bitcast_add_fusion.4
  362.4 1.1 constant_dynamic-slice_fusion.4
  364.5 2.4 bitcast_add_fusion.4
  366.9 1.1 constant_dynamic-slice_fusion.4
  369.0 2.4 bitcast_add_fusion.4
  371.3 1.4 convert_element_type.94
  372.9 1.2 convolution_bitcast_fusion.7
  374.2 1.2 convolution_bitcast_fusion.6
  375.9 1.4 fusion.10
  377.4 5.3 convolution_bitcast_fusion
  382.7 11.3 %copy.88 = f32[2048,1280]{1,0:T(8,128)} copy(f32[2048,1280]{0,1:T(8,128)} %convolution_bitcast_fusion) | data formatting | bytes 20971520
  394.1 110.9 %reduce-scatter.4.cloned.1.call-done = f32[64,1280]{1,0:T(8,128)} async-done(((f32[2048,1280]{1,0:T(8,128)}), f32[64,1280]{1,0:T(8,128)}) %reduce-scatter.4.cloned.1.call-update) | async-done | bytes 327696 | tf_op jit(solution)/shard_map/reduce_scatter | solution.py:152
  505.0 4.3 convolution_bitcast_fusion.1
  509.4 39.4 %all-gather.14.cloned.1.call-done = f32[512,1280]{1,0:T(8,128)} async-done(((f32[64,1280]{1,0:T(8,128)}), f32[512,1280]{1,0:T(8,128)}) %all-gather.14.cloned.1.call-update) | async-done | bytes 2621456 | tf_op jit(solution)/shard_map/all_gather | solution.py:160
  548.7 1.9 reduce_sum.20
  (129 shorter events, 64.0 us)
Async XLA Ops:
  7.2 72.8 %copy-start = (bf16[1,128,2048]{2,1,0:T(8,128)(2,1)S(1)}, bf16[1,128,2048]{2,1,0:T(8,128)(2,1)}, u32[]{:S(2)}) copy-start(bf16[1,128,2048]{2,1,0:T(8,128)(2,1)} %param.9) | copy-start | bytes 1572868
  7.2 58.5 %all-gather.8.cloned.1.call-start = ((), (), s32[]{:S(2)}) async-start(), calls=%async_computation.1 | async-start | bytes 5406720 | tf_op jit(solution)/shard_map/all_gather | solution.py:108
  7.9 152.9 %all-gather.12.cloned.1.call-start = ((), (), s32[]{:S(2)}) async-start(), calls=%async_computation.3 | async-start | bytes 17301504 | tf_op jit(solution)/shard_map/all_gather | solution.py:12
  77.6 2.4 copy-start.1
  79.9 3.4 copy-start.4
  83.3 157.2 %all-gather.10.cloned.1.call-start = ((), (), s32[]{:S(2)}) async-start(), calls=%async_computation.2 | async-start | bytes 17301504 | tf_op jit(solution)/shard_map/all_gather | solution.py:12
  83.6 77.3 %copy-start.2 = (bf16[1,128,1024]{1,2,0:T(8,128)(2,1)}, bf16[1,128,1024]{1,2,0:T(8,128)(2,1)S(1)}, u32[]{:S(2)}) copy-start(bf16[1,128,1024]{1,2,0:T(8,128)(2,1)S(1)} %copy.62) | copy-start | bytes 786436
  85.4 419.6 %reduce-scatter.4.cloned.1.call-start = ((), (), s32[]{:S(2)}) async-start(), calls=%async_computation.5 | async-start | bytes 10813440 | tf_op jit(solution)/shard_map/reduce_scatter | solution.py:152
  106.6 54.3 %copy-start.5 = (pred[128,128]{0,1:T(8,128)(4,1)}, pred[128,128]{0,1:T(8,128)(4,1)S(1)}, u32[]{:S(2)}) copy-start(pred[128,128]{0,1:T(8,128)(4,1)S(1)} %iota_compare_fusion) | copy-start | bytes 49156
  371.3 4.6 copy-start.3
  394.0 154.7 %all-gather.14.cloned.1.call-start = ((), (), s32[]{:S(2)}) async-start(), calls=%async_computation.4 | async-start | bytes 2949120 | tf_op jit(solution)/shard_map/all_gather | solution.py:160
Sparse Core Ops, SparseCore 0:
  10.6 55.0 all-gather.7
  83.4 77.3 all-gather.11
  163.4 77.0 all-gather.9
  394.1 110.8 reduce-scatter.3
  506.8 41.9 all-gather.13
